TPU v7x, 128 devices: a whole 4x4x4 slice. The times are simulated.
128 devices in a mesh: dp: 32 (over z, y, core), mp: 4 (over x).
Axes of the slice: x: 4, y: 4, z: 4, core: 2. Of those that a mesh axis runs over, the one named last changes fastest.
Arguments:
- tokens: bfloat16 [57344, 1024], P('dp'), may hold values from -60 to 60
- segment_ids: int32 [57344], P('dp'), may hold values from 0 to 127, as said below
- page_table: int32 [448], P('dp'), may hold values from 0 to 447, as said below
- w_query: bfloat16 [1024, 1024], P('dp', 'mp'), may hold values from -0.1875 to 0.1875
- w_key: bfloat16 [1024, 1024], P('dp', 'mp'), may hold values from -0.1875 to 0.1875
- w_value: bfloat16 [1024, 1024], P('dp', 'mp'), may hold values from -0.1875 to 0.1875
- w_out: bfloat16 [1024, 1024], P('mp', 'dp'), may hold values from -1.5 to 1.5
- w_up: bfloat16 [1024, 4096], P('dp', 'mp'), may hold values from -0.1875 to 0.1875
- w_down: bfloat16 [4096, 1024], P('mp', 'dp'), may hold values from -0.09375 to 0.09375
- gain_first: float32 [1024], replicated, may hold values from 0.1 to 1.9
- shift_first: float32 [1024], replicated, may hold values from -3 to 3
- gain_second: float32 [1024], replicated, may hold values from 0.1 to 1.9
- shift_second: float32 [1024], replicated, may hold values from -3 to 3
Outputs:
- mixed: bfloat16 [57344, 1024], P('dp')
- kv_cache: bfloat16 [57344, 2, 1024], P('dp', None, 'mp')
Inputs may be any that keep to these rules, and one draw needn't show every extreme that they name: page_table is a permutation of the page slots. Page p lies on device p // 14 in arrival order and goes to device page_table[p] // 14; from one device at most 1 pages go to one device, and some pair reaches 1. `segment_ids`: tokens with equal ids form one request; after dealing, a request's tokens are consecutive and lie on one device, which holds at most 4 requests.
All inputs are finite; a program needn't handle non-finite values.
Results may differ from a plain program's by a relative error of at most 0.014.
Values may be sent and summed in bfloat16 or wider, within the bound.
No kernel may reach another device: no remote copies, remote signals or barrier semaphores. Data moves between devices by JAX's collectives and lax.ppermute only.
A program may use at most 128 MiB of HBM per device.

v0:
```python
import jax
import jax.numpy as jnp
from jax import lax
from jax.sharding import PartitionSpec as P

HEAD = 64


def layer_norm(hidden_sum, gain, shift):
    center = hidden_sum - jnp.mean(hidden_sum, axis=-1, keepdims=True)
    spread = jnp.mean(center * center, axis=-1, keepdims=True)
    return center * lax.rsqrt(spread + 1e-05) * gain + shift


def attend_head(query, keys, values, segments, block_rows):
    blocks = query.shape[0] // block_rows
    query_blocks = query.reshape(blocks, block_rows, query.shape[1])
    segment_blocks = segments.reshape(blocks, block_rows)

    def per_block(bundle):
        rows, row_ids = bundle
        scores = jnp.einsum("qd,kd->qk", rows, keys, preferred_element_type=jnp.float32) * HEAD ** (
            -0.5
        )
        scores = jnp.where(row_ids[:, None] == segments[None, :], scores, -1e30)
        highest = jnp.max(scores, axis=1, keepdims=True)
        raised = jnp.exp(scores - highest)
        attn_weights = (raised / jnp.sum(raised, axis=1, keepdims=True)).astype(jnp.bfloat16)
        return jnp.dot(attn_weights, values, preferred_element_type=jnp.float32).astype(
            jnp.bfloat16
        )

    return lax.map(per_block, (query_blocks, segment_blocks)).reshape(
        query.shape[0], values.shape[1]
    )


def finish(partial_value, residual, gain, shift):
    total = lax.psum(partial_value.astype(jnp.bfloat16), "mp").astype(jnp.float32)
    return layer_norm(residual.astype(jnp.float32) + total, gain, shift).astype(jnp.bfloat16)


def outgoing_pages(source, got_slots, pages_dev, page):
    paged = source.reshape(pages_dev, page, source.shape[1])[jnp.clip(got_slots, 0, pages_dev - 1)]
    return jnp.where((got_slots >= 0)[:, None, None], paged, jnp.zeros_like(paged))


def body(
    tokens,
    segment_ids,
    page_table,
    w_query,
    w_key,
    w_value,
    w_out,
    w_up,
    w_down,
    gain_first,
    shift_first,
    gain_second,
    shift_second,
):
    n_data = lax.axis_size("dp")
    pages_dev = page_table.shape[0]
    page = tokens.shape[0] // pages_dev
    width = tokens.shape[1]
    slots_per = (pages_dev + n_data - 1) // n_data
    buffer_rows = n_data * slots_per
    target = page_table // pages_dev
    local_slot = page_table % pages_dev
    order = jnp.arange(pages_dev, dtype=jnp.int32)
    earlier = (target[:, None] == target[None, :]) & (order[:, None] < order[None, :])
    rank = jnp.sum(earlier.astype(jnp.int32), axis=0)
    position = target * slots_per + rank
    send_ids = (
        jnp.zeros((buffer_rows, page), jnp.int32)
        .at[position]
        .set(segment_ids.reshape(pages_dev, page))
    )
    send_slots = jnp.full((buffer_rows,), -1, jnp.int32).at[position].set(local_slot)
    send_pages = (
        jnp.zeros((buffer_rows, page, width), tokens.dtype)
        .at[position]
        .set(tokens.reshape(pages_dev, page, width))
    )
    got_pages, got_ids, got_slots = (
        lax.all_to_all(send_pages, "dp", split_axis=0, concat_axis=0, tiled=True),
        lax.all_to_all(send_ids, "dp", split_axis=0, concat_axis=0, tiled=True),
        lax.all_to_all(send_slots, "dp", split_axis=0, concat_axis=0, tiled=True),
    )
    matches = got_slots[None, :] == order[:, None]
    source_row = jnp.sum(
        jnp.where(matches, jnp.arange(buffer_rows, dtype=jnp.int32)[None, :], 0), axis=1
    )
    dealt = got_pages[source_row].reshape(pages_dev * page, got_pages.shape[2])
    dealt_ids = got_ids[source_row].reshape(pages_dev * page)
    full_query, full_key, full_value, full_up, full_out, full_down = (
        lax.all_gather(w_query, "dp", axis=0, tiled=True),
        lax.all_gather(w_key, "dp", axis=0, tiled=True),
        lax.all_gather(w_value, "dp", axis=0, tiled=True),
        lax.all_gather(w_up, "dp", axis=0, tiled=True),
        lax.all_gather(w_out, "dp", axis=1, tiled=True),
        lax.all_gather(w_down, "dp", axis=1, tiled=True),
    )
    query = jnp.dot(dealt, full_query, preferred_element_type=jnp.float32).astype(jnp.bfloat16)
    keys = jnp.dot(dealt, full_key, preferred_element_type=jnp.float32).astype(jnp.bfloat16)
    values = jnp.dot(dealt, full_value, preferred_element_type=jnp.float32).astype(jnp.bfloat16)
    suitable = [
        count for count in range(1, pages_dev + 1) if pages_dev % count == 0 and count * page >= 512
    ]
    block_rows = suitable[0] * page
    heads_here = query.shape[1] // HEAD
    contexts = []
    for head in range(heads_here):
        cols = slice(head * HEAD, (head + 1) * HEAD)
        contexts.append(
            attend_head(query[:, cols], keys[:, cols], values[:, cols], dealt_ids, block_rows)
        )
    context = jnp.concatenate(contexts, axis=1)
    partial_value = jnp.dot(context, full_out, preferred_element_type=jnp.float32)
    first = finish(partial_value, dealt, gain_first, shift_first)
    hidden = jax.nn.gelu(
        jnp.dot(first, full_up, preferred_element_type=jnp.float32), approximate=False
    ).astype(jnp.bfloat16)
    second = finish(
        jnp.dot(hidden, full_down, preferred_element_type=jnp.float32),
        first,
        gain_second,
        shift_second,
    )
    returned = lax.all_to_all(
        outgoing_pages(second, got_slots, pages_dev, page),
        "dp",
        split_axis=0,
        concat_axis=0,
        tiled=True,
    )
    mixed = returned[position].reshape(pages_dev * page, width)
    kv_cache = jnp.stack([keys, values], axis=1)
    return (mixed, kv_cache)


def solution(mesh):
    return jax.shard_map(
        body,
        mesh=mesh,
        in_specs=(
            P("dp", None),
            P("dp"),
            P("dp"),
            P("dp", "mp"),
            P("dp", "mp"),
            P("dp", "mp"),
            P("mp", "dp"),
            P("dp", "mp"),
            P("mp", "dp"),
            P(),
            P(),
            P(),
            P(),
        ),
        out_specs=(P("dp", None), P("dp", None, "mp")),
        check_vma=False,
    )
```

profile of v0, /device:TPU:1, one launch (start us, length us, event | category | flops | bytes accessed | tf_op | source)
XLA Modules:
  0.0 659.7 jit_solution(7760421901178392480)
XLA Ops:
  10.1 9.6 %all-to-all-start = ((s32[32,1,1]{2,1,0:T(1,128)}), s32[32,1,1]{2,1,0:T(1,128)S(1)}, u32[]{:S(2)}, u32[]{:S(2)}) async-start(s32[32,1,1]{2,1,0:T(1,128)} %copy.81), calls=%async_computation | async-start | bytes 32768 | tf_op jit(solution)/shard_map/all_to_all | solution.py:89
  20.9 5.7 all-to-all-done
  26.6 4.1 all-to-all-start.2
  30.7 4.3 broadcast.142
  35.0 10.6 %scatter_fusion = bf16[32,128,1024]{2,1,0:T(8,128)(2,1)} fusion(bf16[32,128,1024]{2,1,0:T(8,128)(2,1)} %broadcast.142, s32[14]{0:T(128)S(1)} %compare_select_fusion.2, bf16[14,128,1024]{2,1,0:T(8,128)(2,1)} %bitcast.139), kind=kCustom, calls=%fused_computation.5 | custom fusion | bytes 11010104 | tf_op jit(solution)/shard_map/scatter | solution.py:84
  45.6 7.7 %all-to-all-start.1 = ((bf16[32,128,1024]{2,1,0:T(8,128)(2,1)}), bf16[32,128,1024]{2,1,0:T(8,128)(2,1)}, u32[]{:S(2)}, u32[]{:S(2)}) async-start(bf16[32,128,1024]{2,1,0:T(8,128)(2,1)} %scatter_fusion), calls=%async_computation.1 | async-start | bytes 16777216 | tf_op jit(solution)/shard_map/all_to_all | solution.py:87
  53.4 119.3 %all_gather.19 = bf16[1024,256]{1,0:T(8,128)(2,1)S(1)} all-gather(bf16[32,256]{1,0:T(8,128)(2,1)S(1)} %copy-done.16), channel_id=1, replica_groups=mesh['dp'=32,'mp'=4] {'dp'}, dimensions={0}, use_global_device_ids=true | all-gather | bytes 540672 | tf_op jit(solution)/shard_map/all_gather | solution.py:99
  172.7 25.7 %all_gather.20 = bf16[1024,256]{1,0:T(8,128)(2,1)S(1)} all-gather(bf16[32,256]{1,0:T(8,128)(2,1)S(1)} %copy-done.17), channel_id=1, replica_groups=mesh['dp'=32,'mp'=4] {'dp'}, dimensions={0}, use_global_device_ids=true | all-gather | bytes 540672 | tf_op jit(solution)/shard_map/all_gather | solution.py:100
  198.4 22.1 %all_gather.18 = bf16[1024,256]{1,0:T(8,128)(2,1)S(1)} all-gather(bf16[32,256]{1,0:T(8,128)(2,1)S(1)} %copy-done.18), channel_id=1, replica_groups=mesh['dp'=32,'mp'=4] {'dp'}, dimensions={0}, use_global_device_ids=true | all-gather | bytes 540672 | tf_op jit(solution)/shard_map/all_gather | solution.py:98
  220.5 27.3 %all_gather.21 = bf16[256,1024]{0,1:T(8,128)(2,1)} all-gather(bf16[256,32]{0,1:T(8,128)(2,1)S(1)} %copy-done.19), channel_id=1, replica_groups=mesh['dp'=32,'mp'=4] {'dp'}, dimensions={1}, use_global_device_ids=true | all-gather | bytes 540672 | tf_op jit(solution)/shard_map/all_gather | solution.py:102
  247.8 1.6 clamp_reduce_fusion
  250.2 6.1 gather_fusion
  256.3 3.2 convolution_convert_fusion.3
  261.4 3.2 convolution_convert_fusion.2
  266.6 3.2 convolution_convert_fusion.4
  270.9 7.8 %while.40 = (s32[]{:T(128)}, bf16[2,896,64]{1,2,0:T(8,128)(2,1)S(1)}, s32[2,896]{1,0:T(2,128)S(1)}, s32[14,128]{1,0:T(8,128)S(1)}, bf16[2,896,64]{2,1,0:T(8,128)...) while((s32[]{:T(128)}, bf16[2,896,64]{1,2,0:T(8,128)(2,1)S(1)}, ...), condition=%wide.region_8.9_spmd, body=%wide.region_5.8_spmd.sunk | while | flops 425548032 | bytes 20567648 | solution.py:33
  271.1 1.2 fusion.142
  273.4 1.5 fusion.144
  274.9 1.2 fusion.142
  277.2 1.5 fusion.144
  280.3 7.7 %while.41 = (s32[]{:T(128)}, bf16[2,896,64]{1,2,0:T(8,128)(2,1)S(1)}, s32[2,896]{1,0:T(2,128)S(1)}, s32[14,128]{1,0:T(8,128)S(1)}, bf16[2,896,64]{2,1,0:T(8,128)...) while((s32[]{:T(128)}, bf16[2,896,64]{1,2,0:T(8,128)(2,1)S(1)}, ...), condition=%wide.region_12.13_spmd, body=%wide.region_9.12_spmd.sunk | while | flops 425548032 | bytes 20567648 | solution.py:33
  280.3 1.2 fusion.147
  282.6 1.5 fusion.149
  284.2 1.2 fusion.147
  286.4 1.5 fusion.149
  288.9 7.7 %while.42 = (s32[]{:T(128)}, bf16[2,896,64]{1,2,0:T(8,128)(2,1)S(1)}, s32[2,896]{1,0:T(2,128)S(1)}, s32[14,128]{1,0:T(8,128)S(1)}, bf16[2,896,64]{2,1,0:T(8,128)...) while((s32[]{:T(128)}, bf16[2,896,64]{1,2,0:T(8,128)(2,1)S(1)}, ...), condition=%wide.region_16.17_spmd, body=%wide.region_13.16_spmd.sunk | while | flops 425548032 | bytes 20567648 | solution.py:33
  291.2 1.5 fusion.154
  295.0 1.5 fusion.154
  297.5 7.9 %while.43 = (s32[]{:T(128)}, bf16[2,896,64]{1,2,0:T(8,128)(2,1)S(1)}, s32[2,896]{1,0:T(2,128)S(1)}, s32[14,128]{1,0:T(8,128)S(1)}, bf16[2,896,64]{2,1,0:T(8,128)...) while((s32[]{:T(128)}, bf16[2,896,64]{1,2,0:T(8,128)(2,1)S(1)}, ...), condition=%wide.region_20.21_spmd, body=%wide.region_17.20_spmd.sunk | while | flops 425548032 | bytes 20567648 | solution.py:33
  300.0 1.5 fusion.159
  303.8 1.5 fusion.159
  305.4 3.0 convolution_convert_fusion
  309.7 80.8 %all-reduce.3.cloned.1.call-done = bf16[1792,1024]{1,0:T(8,128)(2,1)} async-done(((bf16[1792,1024]{1,0:T(8,128)(2,1)}), bf16[1792,1024]{1,0:T(8,128)(2,1)}) %all-reduce.3.cloned.1.call-update) | async-done | bytes 3670032 | tf_op jit(solution)/shard_map/psum | solution.py:39
  390.5 4.5 fusion.43
  396.0 2.3 multiply_reduce_fusion.1
  398.3 3.3 add_convert_fusion.1
  401.7 26.1 %convolution_convert_fusion.1 = bf16[1792,1024]{1,0:T(8,128)(2,1)} fusion(bf16[1024,1024]{0,1:T(8,128)(2,1)} %all-gather.5.cloned.1.call-done, bf16[1792,1024]{1,0:T(8,128)(2,1)} %add_convert_fusion.1, bf16[1024,1024]{1,0:T(8,128)(2,1)} %all-gather.3.cloned.1.call-done), kind=kOutput, calls=%fused_computation.86 | convolution fusion | flops 7637303296 | bytes 11534336 | tf_op jit(solution)/shard_map/dot_general | solution.py:126
  428.5 83.4 %all-reduce.5.cloned.1.call-done = bf16[1792,1024]{1,0:T(8,128)(2,1)} async-done(((bf16[1792,1024]{1,0:T(8,128)(2,1)}), bf16[1792,1024]{1,0:T(8,128)(2,1)}) %all-reduce.5.cloned.1.call-update) | async-done | bytes 3670032 | tf_op jit(solution)/shard_map/psum | solution.py:39
  511.9 4.3 fusion.45
  517.2 2.4 multiply_reduce_fusion
  519.7 3.3 add_convert_fusion
  523.1 7.0 %gather_fusion.2 = bf16[32,128,1024]{2,1,0:T(8,128)(2,1)} fusion(bf16[14,128,1024]{2,1,0:T(8,128)(2,1)} %bitcast.136, s32[1024]{0:T(1024)S(1)} %pad_clamp_fusion.1), kind=kCustom, calls=%fused_computation.2 | custom fusion | bytes 16777344 | tf_op jit(solution)/shard_map/gather | solution.py:44
  530.0 7.2 %broadcast_select_fusion = bf16[32,128,1024]{2,1,0:T(8,128)(2,1)} fusion(bf16[32,128,1024]{2,1,0:T(8,128)(2,1)} %gather_fusion.2, pred[32]{0:T(512)(128)(4,1)S(1)} %compare_reduce_fusion), kind=kLoop, calls=%fused_computation.56 | loop fusion | flops 4194304 | bytes 16777248 | tf_op jit(solution)/shard_map/jit(_where)/select_n | solution.py:45
  537.2 8.1 %all-to-all-start.3 = ((bf16[32,128,1024]{2,1,0:T(8,128)(2,1)}), bf16[32,128,1024]{2,1,0:T(8,128)(2,1)}, u32[]{:S(2)}, u32[]{:S(2)}) async-start(bf16[32,128,1024]{2,1,0:T(8,128)(2,1)} %broadcast_select_fusion), calls=%async_computation.3 | async-start | bytes 16777216 | tf_op jit(solution)/shard_map/all_to_all | solution.py:131
  545.3 1.4 pad_maximum_fusion
  546.7 3.6 copy.98
  550.3 95.7 %all-to-all-done.3 = bf16[32,128,1024]{2,1,0:T(8,128)(2,1)} async-done(((bf16[32,128,1024]{2,1,0:T(8,128)(2,1)}), bf16[32,128,1024]{2,1,0:T(8,128)(2,1)}, u32[]{:S(2)}, u32[]{:S(2)}) %all-to-all-start.3) | async-done | bytes 8388640 | tf_op jit(solution)/shard_map/all_to_all | solution.py:131
  646.0 6.0 gather_fusion.3
  (128 shorter events, 29.6 us)
Async XLA Ops:
  8.0 11.7 %copy-start = (s32[1792]{0:T(1024)S(1)}, s32[1792]{0:T(1024)}, u32[]{:S(2)}) copy-start(s32[1792]{0:T(1024)} %param.22) | copy-start | bytes 21508
  8.8 36.8 %copy-start.24 = (s32[14]{0:T(128)}, s32[14]{0:T(128)S(1)}, u32[]{:S(2)}) copy-start(s32[14]{0:T(128)S(1)} %compare_select_fusion.2) | copy-start | bytes 172
  10.1 16.5 %all-to-all-start = ((s32[32,1,1]{2,1,0:T(1,128)}), s32[32,1,1]{2,1,0:T(1,128)S(1)}, u32[]{:S(2)}, u32[]{:S(2)}) async-start(s32[32,1,1]{2,1,0:T(1,128)} %copy.81), calls=%async_computation | async-start | bytes 32768 | tf_op jit(solution)/shard_map/all_to_all | solution.py:89
  26.6 221.2 %copy-start.14 = (s32[32,1,1]{2,1,0:T(1,128)}, s32[32,1,1]{2,1,0:T(1,128)S(1)}, u32[]{:S(2)}) copy-start(s32[32,1,1]{2,1,0:T(1,128)S(1)} %all-to-all-done) | copy-start | bytes 388
  26.6 19.0 %all-to-all-start.2 = ((s32[32,1,128]{2,1,0:T(1,128)}), s32[32,1,128]{2,1,0:T(1,128)S(1)}, u32[]{:S(2)}, u32[]{:S(2)}) async-start(s32[32,1,128]{2,1,0:T(1,128)} %bitcast.18), calls=%async_computation.2 | async-start | bytes 32768 | tf_op jit(solution)/shard_map/all_to_all | solution.py:88
  45.6 7.8 %copy-start.16 = (bf16[32,256]{1,0:T(8,128)(2,1)S(1)}, bf16[32,256]{1,0:T(8,128)(2,1)}, u32[]{:S(2)}) copy-start(bf16[32,256]{1,0:T(8,128)(2,1)} %param.25) | copy-start | bytes 49156
  45.6 127.1 %copy-start.17 = (bf16[32,256]{1,0:T(8,128)(2,1)S(1)}, bf16[32,256]{1,0:T(8,128)(2,1)}, u32[]{:S(2)}) copy-start(bf16[32,256]{1,0:T(8,128)(2,1)} %param.26) | copy-start | bytes 49156
  45.6 152.8 %copy-start.18 = (bf16[32,256]{1,0:T(8,128)(2,1)S(1)}, bf16[32,256]{1,0:T(8,128)(2,1)}, u32[]{:S(2)}) copy-start(bf16[32,256]{1,0:T(8,128)(2,1)} %param.24) | copy-start | bytes 49156
  45.6 174.9 %copy-start.19 = (bf16[256,32]{0,1:T(8,128)(2,1)S(1)}, bf16[256,32]{0,1:T(8,128)(2,1)}, u32[]{:S(2)}) copy-start(bf16[256,32]{0,1:T(8,128)(2,1)} %param.27) | copy-start | bytes 49156
  45.6 204.6 %all-to-all-start.1 = ((bf16[32,128,1024]{2,1,0:T(8,128)(2,1)}), bf16[32,128,1024]{2,1,0:T(8,128)(2,1)}, u32[]{:S(2)}, u32[]{:S(2)}) async-start(bf16[32,128,1024]{2,1,0:T(8,128)(2,1)} %scatter_fusion), calls=%async_computation.1 | async-start | bytes 16777216 | tf_op jit(solution)/shard_map/all_to_all | solution.py:87
  53.3 337.1 %all-reduce.3.cloned.1.call-start = ((), (), s32[]{:S(2)}) async-start(), calls=%async_computation.4 | async-start | bytes 7340032 | tf_op jit(solution)/shard_map/psum | solution.py:39
  259.5 0.9 copy-start.6
  264.7 0.9 copy-start.8
  288.9 7.7 %copy-start.9 = (bf16[1792,64]{0,1:T(8,128)(2,1)S(1)}, bf16[1792,64]{0,1:T(8,128)(2,1)}, u32[]{:S(2)}) copy-start(bf16[1792,64]{0,1:T(8,128)(2,1)} %get-tuple-element.375) | copy-start | bytes 688132
  288.9 8.0 %copy-start.10 = (bf16[1792,64]{0,1:T(8,128)(2,1)S(1)}, bf16[1792,64]{0,1:T(8,128)(2,1)}, u32[]{:S(2)}) copy-start(bf16[1792,64]{0,1:T(8,128)(2,1)} %get-tuple-element.371) | copy-start | bytes 688132
  288.9 8.3 %copy-start.11 = (bf16[1792,64]{0,1:T(8,128)(2,1)S(1)}, bf16[1792,64]{0,1:T(8,128)(2,1)}, u32[]{:S(2)}) copy-start(bf16[1792,64]{0,1:T(8,128)(2,1)} %get-tuple-element.379) | copy-start | bytes 688132
  297.5 7.9 %copy-start.12 = (bf16[256,1024]{0,1:T(8,128)(2,1)S(1)}, bf16[256,1024]{0,1:T(8,128)(2,1)}, u32[]{:S(2)}) copy-start(bf16[256,1024]{0,1:T(8,128)(2,1)} %all_gather.21) | copy-start | bytes 1572868
  297.5 7.9 %copy-start.13 = (bf16[2,8,8,896]{3,2,0,1:T(8,128)(2,1)S(1)}, bf16[2,8,8,896]{3,2,0,1:T(8,128)(2,1)}, u32[]{:S(2)}) copy-start(bf16[2,8,8,896]{3,2,0,1:T(8,128)(2,1)} %copy.103) | copy-start | bytes 688132
  308.4 93.2 %all-gather.3.cloned.1.call-start = ((), (), s32[]{:S(2)}) async-start(), calls=%async_computation.5 | async-start | bytes 2162688 | tf_op jit(solution)/shard_map/all_gather | solution.py:101
  309.0 92.7 %all-gather.5.cloned.1.call-start = ((), (), s32[]{:S(2)}) async-start(), calls=%async_computation.6 | async-start | bytes 2162688 | tf_op jit(solution)/shard_map/all_gather | solution.py:103
  309.6 88.7 %copy-start.20 = (f32[1024]{0:T(1024)S(1)}, f32[1024]{0:T(1024)}, u32[]{:S(2)}) copy-start(f32[1024]{0:T(1024)} %param.31) | copy-start | bytes 12292
  309.6 88.7 %copy-start.21 = (f32[1024]{0:T(1024)S(1)}, f32[1024]{0:T(1024)}, u32[]{:S(2)}) copy-start(f32[1024]{0:T(1024)} %param.30) | copy-start | bytes 12292
  309.6 202.3 %all-reduce.5.cloned.1.call-start = ((), (), s32[]{:S(2)}) async-start(), calls=%async_computation.7 | async-start | bytes 7340032 | tf_op jit(solution)/shard_map/psum | solution.py:39
  390.5 4.5 copy-start.2
  390.5 5.5 copy-start.4
  401.7 26.1 %copy-start.26 = (s32[32]{0:T(128)S(1)}, s32[32]{0:T(128)}, u32[]{:S(2)}) copy-start(s32[32]{0:T(128)} %get-tuple-element.304) | copy-start | bytes 388
  401.7 26.2 %copy-start.15 = (s32[32,1,1]{2,1,0:T(1,128)S(1)}, s32[32,1,1]{2,1,0:T(1,128)}, u32[]{:S(2)}) copy-start(s32[32,1,1]{2,1,0:T(1,128)} %copy-done.14) | copy-start | bytes 388
  428.5 91.2 %copy-start.22 = (f32[1024]{0:T(1024)S(1)}, f32[1024]{0:T(1024)}, u32[]{:S(2)}) copy-start(f32[1024]{0:T(1024)} %param.33) | copy-start | bytes 12292
  428.5 91.2 %copy-start.23 = (f32[1024]{0:T(1024)S(1)}, f32[1024]{0:T(1024)}, u32[]{:S(2)}) copy-start(f32[1024]{0:T(1024)} %param.32) | copy-start | bytes 12292
  511.9 4.3 copy-start.3
  511.9 5.3 copy-start.5
  537.2 8.1 %copy-start.25 = (s32[14]{0:T(128)S(1)}, s32[14]{0:T(128)}, u32[]{:S(2)}) copy-start(s32[14]{0:T(128)} %copy-done.24) | copy-start | bytes 172
  537.2 8.1 %copy-start.7 = (bf16[1792,256]{0,1:T(8,128)(2,1)S(1)}, bf16[1792,256]{0,1:T(8,128)(2,1)}, u32[]{:S(2)}) copy-start(bf16[1792,256]{0,1:T(8,128)(2,1)} %copy-done.6) | copy-start | bytes 2752516
  537.2 108.8 %all-to-all-start.3 = ((bf16[32,128,1024]{2,1,0:T(8,128)(2,1)}), bf16[32,128,1024]{2,1,0:T(8,128)(2,1)}, u32[]{:S(2)}, u32[]{:S(2)}) async-start(bf16[32,128,1024]{2,1,0:T(8,128)(2,1)} %broadcast_select_fusion), calls=%async_computation.3 | async-start | bytes 16777216 | tf_op jit(solution)/shard_map/all_to_all | solution.py:131
  545.3 106.7 %copy-start.1 = (s32[1792]{0:T(1024)S(1)}, s32[1792]{0:T(1024)}, u32[]{:S(2)}) copy-start(s32[1792]{0:T(1024)} %param.22) | copy-start | bytes 21508
Sparse Core Ops, SparseCore 0:
  308.6 81.8 all-reduce.2
  427.9 83.9 all-reduce.4
Sparse Core Ops, SparseCore 1:
  311.2 41.8 all-gather.2
  355.2 42.9 all-gather.4
where the time goes:
time: 670 us; the launch traced here: 660 us
  waiting for transfers between devices  267 us (40%)
  blocking collectives  194 us (29%)
  matrix products  60.7 us (9%)
  local copies, waits for them, and re-layouts  51 us (8%)
  other arithmetic  40.2 us (6%)
  starting transfers between devices  29.6 us (4%)
  between operations  16.2 us (2%)
    psum x2, waiting for transfers between devices, finish(): lax.psum(partial_value.astype(jnp.bfloat16), 'mp').astype(jnp.float32)  164 us
    all_gather x1, blocking collectives, body(): lax.all_gather(w_key, 'dp', axis=0, tiled=True)  119 us
    all_to_all x1, waiting for transfers between devices, body(): lax.all_to_all(outgoing_pages(second, got_slots, pages_dev, page), 'dp',...  95.7 us
    all_gather x1, blocking collectives, body(): lax.all_gather(w_out, 'dp', axis=1, tiled=True)  27.3 us
    dot_general x1, matrix products, body(): jnp.dot(hidden, full_down, preferred_element_type=jnp.float32)  26.1 us
    all_gather x1, blocking collectives, body(): lax.all_gather(w_value, 'dp', axis=0, tiled=True)  25.7 us
    all_gather x1, blocking collectives, body(): lax.all_gather(w_query, 'dp', axis=0, tiled=True)  22.1 us
  transfers between devices with their start and end apart: 8, of which 4 were waited for; matrix products, arithmetic and copies ran while one was open for 5% of the time, Pallas kernels for 0%

commit v1 on v0

v1 whole, which is shorter than its diff:
```python
import jax
import jax.numpy as jnp
from jax import lax
from jax.sharding import PartitionSpec as P

HEAD = 64


def layer_norm(hidden_sum, gain, shift):
    center = hidden_sum - jnp.mean(hidden_sum, axis=-1, keepdims=True)
    spread = jnp.mean(center * center, axis=-1, keepdims=True)
    return center * lax.rsqrt(spread + 1e-05) * gain + shift


def attend_head(query, keys, values, segments, block_rows):
    blocks = query.shape[0] // block_rows
    query_blocks = query.reshape(blocks, block_rows, query.shape[1])
    segment_blocks = segments.reshape(blocks, block_rows)

    def per_block(bundle):
        rows, row_ids = bundle
        scores = jnp.einsum("qd,kd->qk", rows, keys, preferred_element_type=jnp.float32) * HEAD ** (
            -0.5
        )
        scores = jnp.where(row_ids[:, None] == segments[None, :], scores, -1e30)
        highest = jnp.max(scores, axis=1, keepdims=True)
        raised = jnp.exp(scores - highest)
        attn_weights = (raised / jnp.sum(raised, axis=1, keepdims=True)).astype(jnp.bfloat16)
        return jnp.dot(attn_weights, values, preferred_element_type=jnp.float32).astype(
            jnp.bfloat16
        )

    return lax.map(per_block, (query_blocks, segment_blocks)).reshape(
        query.shape[0], values.shape[1]
    )


def body(
    tokens,
    segment_ids,
    page_table,
    w_query,
    w_key,
    w_value,
    w_out,
    w_up,
    w_down,
    gain_first,
    shift_first,
    gain_second,
    shift_second,
):
    n_data = lax.axis_size("dp")
    n_model = lax.axis_size("mp")
    me_model = lax.axis_index("mp")
    pages_dev = page_table.shape[0]
    page = tokens.shape[0] // pages_dev
    width = tokens.shape[1]
    quarter = width // n_model
    sub = page // n_model
    slots_per = (pages_dev + n_data - 1) // n_data
    buffer_rows = n_data * slots_per

    head_cols = w_query.shape[1]
    unit_cols = w_up.shape[1]
    local = jnp.concatenate([w_query, w_key, w_value, w_up, w_out.T, w_down.T], axis=1)
    gathered = lax.all_gather(local, "dp", axis=0, tiled=True)
    at = 0
    full_query = gathered[:, at : at + head_cols]
    at += head_cols
    full_key = gathered[:, at : at + head_cols]
    at += head_cols
    full_value = gathered[:, at : at + head_cols]
    at += head_cols
    full_up = gathered[:, at : at + unit_cols]
    at += unit_cols
    out_t = gathered[:, at : at + w_out.shape[0]]
    at += w_out.shape[0]
    down_t = gathered[:, at : at + w_down.shape[0]]
    out_all_t = lax.all_gather(out_t, "mp", axis=1, tiled=True)

    target = page_table // pages_dev
    local_slot = page_table % pages_dev
    order = jnp.arange(pages_dev, dtype=jnp.int32)
    earlier = (target[:, None] == target[None, :]) & (order[:, None] < order[None, :])
    rank = jnp.sum(earlier.astype(jnp.int32), axis=0)
    position = target * slots_per + rank
    meta = jnp.concatenate(
        [segment_ids.reshape(pages_dev, page), local_slot[:, None]], axis=1
    )
    send_meta = (
        jnp.zeros((buffer_rows, page + 1), jnp.int32).at[:, page].set(-1).at[position].set(meta)
    )
    token_part = lax.dynamic_slice_in_dim(tokens, me_model * quarter, quarter, axis=1)
    send_pages = (
        jnp.zeros((buffer_rows, page, quarter), tokens.dtype)
        .at[position]
        .set(token_part.reshape(pages_dev, page, quarter))
    )
    got_pages = lax.all_to_all(send_pages, "dp", split_axis=0, concat_axis=0, tiled=True)
    got_meta = lax.all_to_all(send_meta, "dp", split_axis=0, concat_axis=0, tiled=True)
    got_ids = got_meta[:, :page]
    got_slots = got_meta[:, page]
    matches = got_slots[None, :] == order[:, None]
    source_row = jnp.sum(
        jnp.where(matches, jnp.arange(buffer_rows, dtype=jnp.int32)[None, :], 0), axis=1
    )
    dealt_part = got_pages[source_row]
    dealt = lax.all_gather(dealt_part, "mp", axis=2, tiled=True).reshape(pages_dev * page, width)
    dealt_ids = got_ids[source_row].reshape(pages_dev * page)

    query = jnp.dot(dealt, full_query, preferred_element_type=jnp.float32).astype(jnp.bfloat16)
    keys = jnp.dot(dealt, full_key, preferred_element_type=jnp.float32).astype(jnp.bfloat16)
    values = jnp.dot(dealt, full_value, preferred_element_type=jnp.float32).astype(jnp.bfloat16)
    suitable = [
        count for count in range(1, pages_dev + 1) if pages_dev % count == 0 and count * page >= 512
    ]
    block_rows = suitable[0] * page
    heads_here = query.shape[1] // HEAD
    contexts = []
    for head in range(heads_here):
        cols = slice(head * HEAD, (head + 1) * HEAD)
        contexts.append(
            attend_head(query[:, cols], keys[:, cols], values[:, cols], dealt_ids, block_rows)
        )
    context = jnp.concatenate(contexts, axis=1)

    context_rows = lax.all_to_all(
        context.reshape(pages_dev, n_model, sub, head_cols),
        "mp",
        split_axis=1,
        concat_axis=1,
        tiled=True,
    )
    attended = jnp.zeros((pages_dev, sub, width), jnp.float32)
    for group in range(n_model):
        term = jnp.einsum(
            "pic,oc->pio",
            context_rows[:, group],
            out_all_t[:, group * head_cols : (group + 1) * head_cols],
            preferred_element_type=jnp.float32,
        ).astype(jnp.bfloat16)
        attended = attended + term.astype(jnp.float32)
    dealt_mine = lax.dynamic_index_in_dim(
        dealt.reshape(pages_dev, n_model, sub, width), me_model, axis=1, keepdims=False
    )
    first_mine = layer_norm(
        dealt_mine.astype(jnp.float32) + attended, gain_first, shift_first
    ).astype(jnp.bfloat16)
    first = lax.all_gather(first_mine, "mp", axis=1).reshape(pages_dev * page, width)

    hidden = jax.nn.gelu(
        jnp.dot(first, full_up, preferred_element_type=jnp.float32), approximate=False
    ).astype(jnp.bfloat16)
    fed_term = jnp.einsum(
        "tu,ou->to", hidden, down_t, preferred_element_type=jnp.float32
    ).astype(jnp.bfloat16)
    fed = lax.psum_scatter(
        fed_term.reshape(pages_dev, n_model, sub, width), "mp", scatter_dimension=1, tiled=True
    ).reshape(pages_dev, sub, width)
    second_mine = layer_norm(
        first_mine.astype(jnp.float32) + fed.astype(jnp.float32), gain_second, shift_second
    ).astype(jnp.bfloat16)

    valid = got_slots >= 0
    outgoing = jnp.where(
        valid[:, None, None],
        second_mine[jnp.clip(got_slots, 0, pages_dev - 1)],
        jnp.zeros((), second_mine.dtype),
    )
    returned = lax.all_to_all(outgoing, "dp", split_axis=0, concat_axis=0, tiled=True)
    mixed_mine = returned[position]
    mixed = lax.all_gather(mixed_mine, "mp", axis=1).reshape(pages_dev * page, width)
    kv_cache = jnp.stack([keys, values], axis=1)
    return (mixed, kv_cache)


def solution(mesh):
    return jax.shard_map(
        body,
        mesh=mesh,
        in_specs=(
            P("dp", None),
            P("dp"),
            P("dp"),
            P("dp", "mp"),
            P("dp", "mp"),
            P("dp", "mp"),
            P("mp", "dp"),
            P("dp", "mp"),
            P("mp", "dp"),
            P(),
            P(),
            P(),
            P(),
        ),
        out_specs=(P("dp", None), P("dp", None, "mp")),
        check_vma=False,
    )
```

time: 670 us -> 480 us (0.72)
  blocking collectives: 194 us -> 0 us
  waiting for transfers between devices: 267 us -> 304 us
  other arithmetic: 40.2 us -> 24 us
  local copies, waits for them, and re-layouts: 51 us -> 38.6 us
    all_gather x4 -> x0, blocking collectives: 194 us -> none  [the longest x1 119 us: body(): lax.all_gather(w_key, 'dp', axis=0, tiled=True)]
    all_gather x2 -> x5, waiting for transfers between devices: 0.01 us -> 184 us  [the longest x1 54.7 us: body(): gathered = lax.all_gather(local, 'dp', axis=0, tiled=True)]
    psum x2 -> x0, waiting for transfers between devices: 164 us -> none  [finish(): lax.psum(partial_value.astype(jnp.bfloat16), 'mp').astype(jnp.float32)]
    all_to_all x3, waiting for transfers between devices: 101 us -> 49.1 us  [the longest x1 28.5 us: body(): lax.all_to_all(outgoing, 'dp', split_axis=0, concat_axis=0, tiled=True)]
    reduce_scatter x0 -> x1, waiting for transfers between devices: none -> 43 us  [body(): lax.psum_scatter(fed_term.reshape(pages_dev, n_model, sub, width), 'mp',...]
    all_to_all x1, waiting for transfers between devices: 0.01 us -> 27.3 us  [body(): lax.all_to_all(send_pages, 'dp', split_axis=0, concat_axis=0, tiled=True)]
    gather x3, local copies, waits for them, and re-layouts: 19.1 us -> 5.08 us  [the longest x1 2 us: body(): second_mine[jnp.clip(got_slots, 0, pages_dev - 1)]]
    scatter x3 -> x2, local copies, waits for them, and re-layouts: 12.4 us -> 3.53 us  [the longest x1 2.85 us: body(): send_pages = jnp.zeros((buffer_rows, page, quarter), tokens.dtype).at[pos...]
  transfers between devices with their start and end apart: 8 -> 10, of which waited for: 4 -> 10; matrix products, arithmetic and copies ran while one was open for 5% -> 5% of each run, Pallas kernels for 0% -> 0%
where the time goes in v1:
time: 480 us; the launch traced here: 474 us
  waiting for transfers between devices  304 us (63%)
  matrix products  64.7 us (13%)
  local copies, waits for them, and re-layouts  38.6 us (8%)
  starting transfers between devices  27.4 us (6%)
  other arithmetic  24 us (5%)
  between operations  15.2 us (3%)
    all_gather x1, waiting for transfers between devices, body(): gathered = lax.all_gather(local, 'dp', axis=0, tiled=True)  54.7 us
    all_gather x1, waiting for transfers between devices, body(): lax.all_gather(first_mine, 'mp', axis=1).reshape(pages_dev * page, width)  44.9 us
    reduce_scatter x1, waiting for transfers between devices, body(): lax.psum_scatter(fed_term.reshape(pages_dev, n_model, sub, width), 'mp',...  43 us
    all_gather x1, waiting for transfers between devices, body(): lax.all_gather(dealt_part, 'mp', axis=2, tiled=True)  42.6 us
    all_gather x1, waiting for transfers between devices, body(): lax.all_gather(mixed_mine, 'mp', axis=1).reshape(pages_dev * page, width)  35.7 us
    all_to_all x1, waiting for transfers between devices, body(): lax.all_to_all(outgoing, 'dp', split_axis=0, concat_axis=0, tiled=True)  28.5 us
    all_to_all x1, waiting for transfers between devices, body(): lax.all_to_all(send_pages, 'dp', split_axis=0, concat_axis=0, tiled=True)  27.3 us
    dot_general x1, matrix products, body(): jnp.einsum('tu,ou->to', hidden, down_t, preferred_element_type=jnp.float32)  26.2 us
  transfers between devices with their start and end apart: 10, of which 10 were waited for; matrix products, arithmetic and copies ran while one was open for 5% of the time, Pallas kernels for 0%

profile of v1, /device:TPU:1, one launch (start us, length us, event | category | flops | bytes accessed | tf_op | source)
XLA Modules:
  0.0 474.3 jit_solution(7659568354544722614)
XLA Ops:
  10.2 9.6 %all-to-all-start = ((s32[32,1,129]{2,1,0:T(1,128)}), s32[32,1,129]{2,1,0:T(1,128)S(1)}, u32[]{:S(2)}, u32[]{:S(2)}) async-start(s32[32,1,129]{2,1,0:T(1,128)} %all_to_all.17), calls=%async_computation | async-start | bytes 65536 | tf_op jit(solution)/shard_map/all_to_all | solution.py:101
  21.1 1.6 broadcast_in_dim.96
  22.7 2.8 scatter_fusion
  25.5 1.5 all-to-all-done
  27.1 5.9 %all-to-all-start.1 = ((bf16[32,128,256]{2,1,0:T(8,128)(2,1)}), bf16[32,128,256]{2,1,0:T(8,128)(2,1)S(1)}, u32[]{:S(2)}, u32[]{:S(2)}) async-start(bf16[32,128,256]{2,1,0:T(8,128)(2,1)} %scatter_fusion), calls=%async_computation.1 | async-start | bytes 4194304 | tf_op jit(solution)/shard_map/all_to_all | solution.py:100
  34.2 27.3 %all-to-all-done.1 = bf16[32,128,256]{2,1,0:T(8,128)(2,1)S(1)} async-done(((bf16[32,128,256]{2,1,0:T(8,128)(2,1)}), bf16[32,128,256]{2,1,0:T(8,128)(2,1)S(1)}, u32[]{:S(2)}, u32[]{:S(2)}) %all-to-all-start.1) | async-done | bytes 2097184 | tf_op jit(solution)/shard_map/all_to_all | solution.py:100
  61.5 1.5 gather_fusion
  64.6 42.6 %all-gather.13.cloned.1.call-done = bf16[14,128,1024]{2,1,0:T(8,128)(2,1)} async-done(((bf16[14,128,256]{2,1,0:T(8,128)(2,1)}), bf16[14,128,1024]{2,1,0:T(8,128)(2,1)}) %all-gather.13.cloned.1.call-update) | async-done | bytes 3670032 | tf_op jit(solution)/shard_map/all_gather | solution.py:109
  107.2 54.7 %all-gather.9.cloned.1.call-done = bf16[1024,3072]{1,0:T(8,128)(2,1)} async-done(((bf16[32,3072]{1,0:T(8,128)(2,1)}), bf16[1024,3072]{1,0:T(8,128)(2,1)}) %all-gather.9.cloned.1.call-update) | async-done | bytes 6291472 | tf_op jit(solution)/shard_map/all_gather | solution.py:67
  162.0 3.3 convolution_convert_fusion.2
  167.2 3.3 convolution_convert_fusion.1
  172.6 3.3 convolution_convert_fusion.3
  176.9 7.8 %while.41 = (s32[]{:T(128)}, bf16[2,896,64]{1,2,0:T(8,128)(2,1)S(1)}, s32[2,896]{1,0:T(2,128)S(1)}, s32[14,128]{1,0:T(8,128)S(1)}, bf16[2,896,64]{2,1,0:T(8,128)...) while((s32[]{:T(128)}, bf16[2,896,64]{1,2,0:T(8,128)(2,1)S(1)}, ...), condition=%wide.region_7.8_spmd, body=%wide.region_4.7_spmd.sunk | while | flops 425548032 | bytes 20567648 | solution.py:33
  179.4 1.5 fusion.137
  183.2 1.5 fusion.137
  186.6 7.7 %while.42 = (s32[]{:T(128)}, bf16[2,896,64]{1,2,0:T(8,128)(2,1)S(1)}, s32[2,896]{1,0:T(2,128)S(1)}, s32[14,128]{1,0:T(8,128)S(1)}, bf16[2,896,64]{2,1,0:T(8,128)...) while((s32[]{:T(128)}, bf16[2,896,64]{1,2,0:T(8,128)(2,1)S(1)}, ...), condition=%wide.region_11.12_spmd, body=%wide.region_8.11_spmd.sunk | while | flops 425548032 | bytes 20567648 | solution.py:33
  188.9 1.5 fusion.142
  192.8 1.5 fusion.142
  195.5 7.9 %while.43 = (s32[]{:T(128)}, bf16[2,896,64]{1,2,0:T(8,128)(2,1)S(1)}, s32[2,896]{1,0:T(2,128)S(1)}, s32[14,128]{1,0:T(8,128)S(1)}, bf16[2,896,64]{2,1,0:T(8,128)...) while((s32[]{:T(128)}, bf16[2,896,64]{1,2,0:T(8,128)(2,1)S(1)}, ...), condition=%wide.region_15.16_spmd, body=%wide.region_12.15_spmd.sunk | while | flops 425548032 | bytes 20567648 | solution.py:33
  197.8 1.5 fusion.147
  201.6 1.5 fusion.147
  204.5 1.9 slice.152
  206.4 7.7 %while.44 = (s32[]{:T(128)}, bf16[2,896,64]{1,2,0:T(8,128)(2,1)S(1)}, s32[2,896]{1,0:T(2,128)S(1)}, s32[14,128]{1,0:T(8,128)S(1)}, bf16[2,896,64]{2,1,0:T(8,128)...) while((s32[]{:T(128)}, bf16[2,896,64]{1,2,0:T(8,128)(2,1)S(1)}, ...), condition=%wide.region_19.20_spmd, body=%wide.region_16.19_spmd.sunk | while | flops 425548032 | bytes 20567648 | solution.py:33
  208.7 1.5 fusion.152
  212.5 1.5 fusion.152
  215.9 4.0 all-to-all-start.2
  219.9 19.1 %all-to-all-done.2 = bf16[14,4,32,256]{3,2,0,1:T(8,128)(2,1)S(1)} async-done(((bf16[14,4,32,256]{3,2,0,1:T(8,128)(2,1)}), bf16[14,4,32,256]{3,2,0,1:T(8,128)(2,1)S(1)}, u32[]{:S(2)}, u32[]{:S(2)}) %all-to-all-start.2) | async-done | bytes 917536 | tf_op jit(solution)/shard_map/all_to_all | solution.py:128
  239.0 6.3 %all-gather.11.cloned.1.call-done = bf16[1024,1024]{1,0:T(8,128)(2,1)} async-done(((bf16[1024,256]{1,0:T(8,128)(2,1)}), bf16[1024,1024]{1,0:T(8,128)(2,1)}) %all-gather.11.cloned.1.call-update) | async-done | bytes 2097168 | tf_op jit(solution)/shard_map/all_gather | solution.py:80
  245.4 1.5 convolution_convert_fusion.7
  246.9 1.5 convolution_convert_fusion.6
  248.3 1.5 convolution_convert_fusion.5
  249.8 2.2 fusion.100
  253.7 44.9 %all-gather.15.cloned.1.call-done = bf16[14,128,1024]{2,1,0:T(8,128)(2,1)} async-done(((bf16[14,32,1024]{2,1,0:T(8,128)(2,1)}), bf16[14,128,1024]{2,1,0:T(8,128)(2,1)}) %all-gather.15.cloned.1.call-update) | async-done | bytes 3670032 | tf_op jit(solution)/shard_map/all_gather | solution.py:150
  298.6 26.2 %convolution_convert_fusion = bf16[1792,1024]{1,0:T(8,128)(2,1)} fusion(bf16[1024,3072]{1,0:T(8,128)(2,1)} %all-gather.9.cloned.1.call-done, bf16[1792,1024]{1,0:T(8,128)(2,1)} %bitcast.184), kind=kOutput, calls=%fused_computation.73 | convolution fusion | flops 7637303296 | bytes 11534336 | tf_op jit(solution)/shard_map/tu,ou->to/dot_general | solution.py:155
  324.8 4.5 copy.99
  329.4 43.0 %reduce-scatter.2.cloned.1.call-done = bf16[14,1,32,1024]{3,2,0,1:T(8,128)(2,1)} async-done(((bf16[14,4,32,1024]{3,2,0,1:T(8,128)(2,1)}), bf16[14,1,32,1024]{3,2,0,1:T(8,128)(2,1)}) %reduce-scatter.2.cloned.1.call-update) | async-done | bytes 917520 | tf_op jit(solution)/shard_map/reduce_scatter | solution.py:158
  372.4 1.8 fusion.51
  374.2 1.9 multiply_reduce_fusion
  376.1 2.8 add_convert_fusion
  379.0 2.0 gather_fusion.2
  381.0 3.2 broadcast_select_fusion
  384.2 7.8 %all-to-all-start.3 = ((bf16[32,32,1024]{2,1,0:T(8,128)(2,1)}), bf16[32,32,1024]{2,1,0:T(8,128)(2,1)S(1)}, u32[]{:S(2)}, u32[]{:S(2)}) async-start(bf16[32,32,1024]{2,1,0:T(8,128)(2,1)} %broadcast_select_fusion), calls=%async_computation.4 | async-start | bytes 4194304 | tf_op jit(solution)/shard_map/all_to_all | solution.py:171
  392.1 28.5 %all-to-all-done.3 = bf16[32,32,1024]{2,1,0:T(8,128)(2,1)S(1)} async-done(((bf16[32,32,1024]{2,1,0:T(8,128)(2,1)}), bf16[32,32,1024]{2,1,0:T(8,128)(2,1)S(1)}, u32[]{:S(2)}, u32[]{:S(2)}) %all-to-all-start.3) | async-done | bytes 2097184 | tf_op jit(solution)/shard_map/all_to_all | solution.py:171
  420.6 1.5 gather_fusion.3
  422.2 1.3 pad_maximum_fusion
  423.5 3.6 copy.100
  427.1 35.7 %all-gather.17.cloned.1.call-done = bf16[14,128,1024]{2,1,0:T(8,128)(2,1)} async-done(((bf16[14,32,1024]{2,1,0:T(8,128)(2,1)}), bf16[14,128,1024]{2,1,0:T(8,128)(2,1)}) %all-gather.17.cloned.1.call-update) | async-done | bytes 3670032 | tf_op jit(solution)/shard_map/all_gather | solution.py:173
  462.7 4.2 copy.146
  (138 shorter events, 37.9 us)
Async XLA Ops:
  7.9 19.1 %copy-start.18 = (s32[14]{0:T(128)}, s32[14]{0:T(128)S(1)}, u32[]{:S(2)}) copy-start(s32[14]{0:T(128)S(1)} %compare_select_fusion.2) | copy-start | bytes 172
  10.2 16.9 %all-to-all-start = ((s32[32,1,129]{2,1,0:T(1,128)}), s32[32,1,129]{2,1,0:T(1,128)S(1)}, u32[]{:S(2)}, u32[]{:S(2)}) async-start(s32[32,1,129]{2,1,0:T(1,128)} %all_to_all.17), calls=%async_computation | async-start | bytes 65536 | tf_op jit(solution)/shard_map/all_to_all | solution.py:101
  21.1 42.1 %copy-start.12 = (bf16[32,256]{1,0:T(8,128)(2,1)S(1)}, bf16[32,256]{1,0:T(8,128)(2,1)}, u32[]{:S(2)}) copy-start(bf16[32,256]{1,0:T(8,128)(2,1)} %param.26) | copy-start | bytes 49156
  21.1 42.1 %copy-start.13 = (bf16[32,256]{1,0:T(8,128)(2,1)S(1)}, bf16[32,256]{1,0:T(8,128)(2,1)}, u32[]{:S(2)}) copy-start(bf16[32,256]{1,0:T(8,128)(2,1)} %param.27) | copy-start | bytes 49156
  21.1 42.1 %copy-start.14 = (bf16[32,256]{1,0:T(8,128)(2,1)S(1)}, bf16[32,256]{1,0:T(8,128)(2,1)}, u32[]{:S(2)}) copy-start(bf16[32,256]{1,0:T(8,128)(2,1)} %param.28) | copy-start | bytes 49156
  21.1 42.1 %copy-start.10 = (bf16[32,1024]{1,0:T(8,128)(2,1)S(1)}, bf16[32,1024]{1,0:T(8,128)(2,1)}, u32[]{:S(2)}) copy-start(bf16[32,1024]{1,0:T(8,128)(2,1)} %param.30) | copy-start | bytes 196612
  21.1 42.1 %copy-start.15 = (bf16[256,32]{0,1:T(8,128)(2,1)S(1)}, bf16[256,32]{0,1:T(8,128)(2,1)}, u32[]{:S(2)}) copy-start(bf16[256,32]{0,1:T(8,128)(2,1)} %param.29) | copy-start | bytes 49156
  21.1 42.1 %copy-start.11 = (bf16[1024,32]{0,1:T(8,128)(2,1)S(1)}, bf16[1024,32]{0,1:T(8,128)(2,1)}, u32[]{:S(2)}) copy-start(bf16[1024,32]{0,1:T(8,128)(2,1)} %param.31) | copy-start | bytes 196612
  27.1 34.5 %all-to-all-start.1 = ((bf16[32,128,256]{2,1,0:T(8,128)(2,1)}), bf16[32,128,256]{2,1,0:T(8,128)(2,1)S(1)}, u32[]{:S(2)}, u32[]{:S(2)}) async-start(bf16[32,128,256]{2,1,0:T(8,128)(2,1)} %scatter_fusion), calls=%async_computation.1 | async-start | bytes 4194304 | tf_op jit(solution)/shard_map/all_to_all | solution.py:100
  32.9 74.3 %all-gather.13.cloned.1.call-start = ((), (), s32[]{:S(2)}) async-start(), calls=%async_computation.8 | async-start | bytes 4587520 | tf_op jit(solution)/shard_map/all_gather | solution.py:109
  33.6 0.6 copy-start.21
  63.1 98.9 %all-gather.9.cloned.1.call-start = ((), (), s32[]{:S(2)}) async-start(), calls=%async_computation.5 | async-start | bytes 6488064 | tf_op jit(solution)/shard_map/all_gather | solution.py:67
  63.3 0.7 copy-start.7
  64.0 181.4 %all-gather.11.cloned.1.call-start = ((), (), s32[]{:S(2)}) async-start(), calls=%async_computation.6 | async-start | bytes 2621440 | tf_op jit(solution)/shard_map/all_gather | solution.py:80
  165.3 0.9 copy-start
  170.6 1.0 copy-start.2
  195.4 8.2 %copy-start.4 = (bf16[1792,64]{0,1:T(8,128)(2,1)S(1)}, bf16[1792,64]{0,1:T(8,128)(2,1)}, u32[]{:S(2)}) copy-start(bf16[1792,64]{0,1:T(8,128)(2,1)} %get-tuple-element.357) | copy-start | bytes 688132
  195.4 8.5 %copy-start.5 = (bf16[1792,64]{0,1:T(8,128)(2,1)S(1)}, bf16[1792,64]{0,1:T(8,128)(2,1)}, u32[]{:S(2)}) copy-start(bf16[1792,64]{0,1:T(8,128)(2,1)} %get-tuple-element.353) | copy-start | bytes 688132
  195.4 8.7 %copy-start.6 = (bf16[1792,64]{0,1:T(8,128)(2,1)S(1)}, bf16[1792,64]{0,1:T(8,128)(2,1)}, u32[]{:S(2)}) copy-start(bf16[1792,64]{0,1:T(8,128)(2,1)} %get-tuple-element.361) | copy-start | bytes 688132
  206.4 8.0 %copy-start.3 = (bf16[2,896,64]{2,1,0:T(8,128)(2,1)S(1)}, bf16[2,896,64]{2,1,0:T(8,128)(2,1)}, u32[]{:S(2)}) copy-start(bf16[2,896,64]{2,1,0:T(8,128)(2,1)} %copy.82) | copy-start | bytes 688132
  215.9 23.1 %all-to-all-start.2 = ((bf16[14,4,32,256]{3,2,0,1:T(8,128)(2,1)}), bf16[14,4,32,256]{3,2,0,1:T(8,128)(2,1)S(1)}, u32[]{:S(2)}, u32[]{:S(2)}) async-start(bf16[14,4,32,256]{3,2,0,1:T(8,128)(2,1)} %copy.105), calls=%async_computation.2 | async-start | bytes 1835008 | tf_op jit(solution)/shard_map/all_to_all | solution.py:128
  219.9 78.7 %all-gather.15.cloned.1.call-start = ((), (), s32[]{:S(2)}) async-start(), calls=%async_computation.9 | async-start | bytes 4587520 | tf_op jit(solution)/shard_map/all_gather | solution.py:150
  219.9 32.4 %copy-start.8 = (f32[1024]{0:T(1024)S(1)}, f32[1024]{0:T(1024)}, u32[]{:S(2)}) copy-start(f32[1024]{0:T(1024)} %param.33) | copy-start | bytes 12292
  219.9 32.4 %copy-start.9 = (f32[1024]{0:T(1024)S(1)}, f32[1024]{0:T(1024)}, u32[]{:S(2)}) copy-start(f32[1024]{0:T(1024)} %param.32) | copy-start | bytes 12292
  253.7 118.7 %reduce-scatter.2.cloned.1.call-start = ((), (), s32[]{:S(2)}) async-start(), calls=%async_computation.7 | async-start | bytes 4587520 | tf_op jit(solution)/shard_map/reduce_scatter | solution.py:158
  324.8 4.6 copy-start.20
  324.8 4.6 copy-start.22
  329.3 46.8 %copy-start.16 = (f32[1024]{0:T(1024)S(1)}, f32[1024]{0:T(1024)}, u32[]{:S(2)}) copy-start(f32[1024]{0:T(1024)} %param.35) | copy-start | bytes 12292
  329.3 46.8 %copy-start.17 = (f32[1024]{0:T(1024)S(1)}, f32[1024]{0:T(1024)}, u32[]{:S(2)}) copy-start(f32[1024]{0:T(1024)} %param.34) | copy-start | bytes 12292
  379.0 13.1 %copy-start.19 = (s32[14]{0:T(128)S(1)}, s32[14]{0:T(128)}, u32[]{:S(2)}) copy-start(s32[14]{0:T(128)} %copy-done.18) | copy-start | bytes 172
  381.0 41.1 %copy-start.1 = (bf16[1792,256]{0,1:T(8,128)(2,1)S(1)}, bf16[1792,256]{0,1:T(8,128)(2,1)}, u32[]{:S(2)}) copy-start(bf16[1792,256]{0,1:T(8,128)(2,1)} %copy-done) | copy-start | bytes 2752516
  384.2 36.4 %all-to-all-start.3 = ((bf16[32,32,1024]{2,1,0:T(8,128)(2,1)}), bf16[32,32,1024]{2,1,0:T(8,128)(2,1)S(1)}, u32[]{:S(2)}, u32[]{:S(2)}) async-start(bf16[32,32,1024]{2,1,0:T(8,128)(2,1)} %broadcast_select_fusion), calls=%async_computation.4 | async-start | bytes 4194304 | tf_op jit(solution)/shard_map/all_to_all | solution.py:171
  392.0 70.7 %all-gather.17.cloned.1.call-start = ((), (), s32[]{:S(2)}) async-start(), calls=%async_computation.10 | async-start | bytes 4587520 | tf_op jit(solution)/shard_map/all_gather | solution.py:173
Sparse Core Ops, SparseCore 0:
  63.2 43.9 all-gather.12
  110.0 51.8 all-gather.8
  206.5 38.8 all-gather.10
  253.8 44.7 all-gather.14
  329.5 42.8 reduce-scatter.1
  422.3 40.4 all-gather.16

commit v2 on v1

--- a/solution.py
+++ b/solution.py
@@ -62,22 +62,21 @@
     buffer_rows = n_data * slots_per
 
     head_cols = w_query.shape[1]
-    unit_cols = w_up.shape[1]
-    local = jnp.concatenate([w_query, w_key, w_value, w_up, w_out.T, w_down.T], axis=1)
-    gathered = lax.all_gather(local, "dp", axis=0, tiled=True)
-    at = 0
-    full_query = gathered[:, at : at + head_cols]
-    at += head_cols
-    full_key = gathered[:, at : at + head_cols]
-    at += head_cols
-    full_value = gathered[:, at : at + head_cols]
-    at += head_cols
-    full_up = gathered[:, at : at + unit_cols]
-    at += unit_cols
-    out_t = gathered[:, at : at + w_out.shape[0]]
-    at += w_out.shape[0]
-    down_t = gathered[:, at : at + w_down.shape[0]]
-    out_all_t = lax.all_gather(out_t, "mp", axis=1, tiled=True)
+    in_part = w_out.shape[0]
+    unit_part = w_up.shape[1]
+    small = jnp.concatenate([w_out.T, w_up, w_down.T], axis=1)
+    small_all = lax.all_gather(small, "mp", axis=1)
+    rows_dp = small.shape[0]
+    out_rows = small_all[:, :, :in_part].reshape(rows_dp, n_model * in_part)
+    up_rows = small_all[:, :, in_part : in_part + unit_part].reshape(rows_dp, n_model * unit_part)
+    down_rows = small_all[:, :, in_part + unit_part :].reshape(rows_dp, n_model * unit_part)
+    attn_local = jnp.concatenate([w_query, w_key, w_value, out_rows], axis=1)
+    attn_gathered = lax.all_gather(attn_local, "dp", axis=0, tiled=True)
+    full_query = attn_gathered[:, :head_cols]
+    full_key = attn_gathered[:, head_cols : 2 * head_cols]
+    full_value = attn_gathered[:, 2 * head_cols : 3 * head_cols]
+    out_all_t = attn_gathered[:, 3 * head_cols :]
+    ffn_local = jnp.concatenate([up_rows, down_rows], axis=1)
 
     target = page_table // pages_dev
     local_slot = page_table % pages_dev
@@ -106,8 +105,14 @@
         jnp.where(matches, jnp.arange(buffer_rows, dtype=jnp.int32)[None, :], 0), axis=1
     )
     dealt_part = got_pages[source_row]
+    dealt_part, attn_gathered = lax.optimization_barrier((dealt_part, attn_gathered))
     dealt = lax.all_gather(dealt_part, "mp", axis=2, tiled=True).reshape(pages_dev * page, width)
     dealt_ids = got_ids[source_row].reshape(pages_dev * page)
+    ffn_local, dealt = lax.optimization_barrier((ffn_local, dealt))
+    ffn_gathered = lax.all_gather(ffn_local, "dp", axis=0, tiled=True)
+    units = n_model * unit_part
+    full_up = ffn_gathered[:, :units]
+    down_t = ffn_gathered[:, units:]
 
     query = jnp.dot(dealt, full_query, preferred_element_type=jnp.float32).astype(jnp.bfloat16)
     keys = jnp.dot(dealt, full_key, preferred_element_type=jnp.float32).astype(jnp.bfloat16)
@@ -147,20 +152,22 @@
     first_mine = layer_norm(
         dealt_mine.astype(jnp.float32) + attended, gain_first, shift_first
     ).astype(jnp.bfloat16)
-    first = lax.all_gather(first_mine, "mp", axis=1).reshape(pages_dev * page, width)
-
     hidden = jax.nn.gelu(
-        jnp.dot(first, full_up, preferred_element_type=jnp.float32), approximate=False
+        jnp.einsum("pid,du->piu", first_mine, full_up, preferred_element_type=jnp.float32),
+        approximate=False,
     ).astype(jnp.bfloat16)
-    fed_term = jnp.einsum(
-        "tu,ou->to", hidden, down_t, preferred_element_type=jnp.float32
-    ).astype(jnp.bfloat16)
-    fed = lax.psum_scatter(
-        fed_term.reshape(pages_dev, n_model, sub, width), "mp", scatter_dimension=1, tiled=True
-    ).reshape(pages_dev, sub, width)
-    second_mine = layer_norm(
-        first_mine.astype(jnp.float32) + fed.astype(jnp.float32), gain_second, shift_second
-    ).astype(jnp.bfloat16)
+    fed = jnp.zeros((pages_dev, sub, width), jnp.float32)
+    for group in range(n_model):
+        term = jnp.einsum(
+            "piu,ou->pio",
+            hidden[:, :, group * unit_part : (group + 1) * unit_part],
+            down_t[:, group * unit_part : (group + 1) * unit_part],
+            preferred_element_type=jnp.float32,
+        ).astype(jnp.bfloat16)
+        fed = fed + term.astype(jnp.float32)
+    second_mine = layer_norm(first_mine.astype(jnp.float32) + fed, gain_second, shift_second).astype(
+        jnp.bfloat16
+    )
 
     valid = got_slots >= 0
     outgoing = jnp.where(

time: 480 us -> 342 us (0.71)
  waiting for transfers between devices: 304 us -> 156 us
  blocking collectives: 0 us -> 12.4 us
  loops' own time: 0.6 us -> 12.3 us
  local copies, waits for them, and re-layouts: 38.6 us -> 31 us
  other arithmetic: 24 us -> 18.3 us
    all_gather x3 -> x2, waiting for transfers between devices: 106 us -> 0.02 us  [the longest x1 0.02 us: body(): ffn_gathered = lax.all_gather(ffn_local, 'dp', axis=0, tiled=True)]
    reduce_scatter x1 -> x0, waiting for transfers between devices: 43 us -> none  [body(): lax.psum_scatter(fed_term.reshape(pages_dev, n_model, sub, width), 'mp',...]
    all_gather x0 -> x1, blocking collectives: none -> 12.4 us  [body(): small_all = lax.all_gather(small, 'mp', axis=1)]
    another operation x4, loops' own time: 0.6 us -> 12.3 us  [attend_head(): lax.map(per_block, (query_blocks, segment_blocks))]
    all_to_all x1, waiting for transfers between devices: 19.1 us -> 11.1 us  [body(): lax.all_to_all(context.reshape(pages_dev, n_model, sub, head_cols), 'mp',...]
    all_to_all x1, waiting for transfers between devices: 27.3 us -> 33.9 us  [body(): lax.all_to_all(send_pages, 'dp', split_axis=0, concat_axis=0, tiled=True)]
    dot_general x1 -> x5, matrix products: 26.2 us -> 26.8 us  [the longest x1 21.7 us: body(): jnp.einsum('pid,du->piu', first_mine, full_up, preferred_element_type=jnp...]
    unnamed x54 -> x40, local copies, waits for them, and re-layouts: 11 us -> 10.4 us
  transfers between devices with their start and end apart: 10 -> 8, of which waited for: 10 -> 6; matrix products, arithmetic and copies ran while one was open for 5% -> 22% of each run, Pallas kernels for 0% -> 0%
where the time goes in v2:
time: 342 us; the launch traced here: 341 us
  waiting for transfers between devices  156 us (46%)
  matrix products  65.3 us (19%)
  local copies, waits for them, and re-layouts  31 us (9%)
  starting transfers between devices  30.7 us (9%)
  other arithmetic  18.3 us (5%)
  between operations  14.6 us (4%)
  blocking collectives  12.4 us (4%)
  loops' own time  12.3 us (4%)
    all_gather x1, waiting for transfers between devices, body(): lax.all_gather(dealt_part, 'mp', axis=2, tiled=True)  45.3 us
    all_gather x1, waiting for transfers between devices, body(): lax.all_gather(mixed_mine, 'mp', axis=1).reshape(pages_dev * page, width)  35.4 us
    all_to_all x1, waiting for transfers between devices, body(): lax.all_to_all(send_pages, 'dp', split_axis=0, concat_axis=0, tiled=True)  33.9 us
    all_to_all x1, waiting for transfers between devices, body(): lax.all_to_all(outgoing, 'dp', split_axis=0, concat_axis=0, tiled=True)  28.5 us
    dot_general x1, matrix products, body(): jnp.einsum('pid,du->piu', first_mine, full_up, preferred_element_type=jnp...  21.7 us
    all_gather x1, blocking collectives, body(): small_all = lax.all_gather(small, 'mp', axis=1)  12.4 us
    another operation x4, loops' own time, attend_head(): lax.map(per_block, (query_blocks, segment_blocks))  12.3 us
    dot_general x8, matrix products, per_block(): jnp.dot(attn_weights, values, preferred_element_type=jnp.float32)  12.2 us
  transfers between devices with their start and end apart: 8, of which 6 were waited for; matrix products, arithmetic and copies ran while one was open for 22% of the time, Pallas kernels for 0%

profile of v2, /device:TPU:1, one launch (start us, length us, event | category | flops | bytes accessed | tf_op | source)
XLA Modules:
  0.0 340.5 jit_solution(8470638990917171062)
XLA Ops:
  8.1 12.4 %all-gather = bf16[32,9216]{1,0:T(8,128)(2,1)S(1)} all-gather(bf16[32,2304]{1,0:T(8,128)(2,1)S(1)} %pad_maximum_fusion.3), channel_id=2, replica_groups=mesh['dp'=32,'mp'=4] {'mp'}, dimensions={1}, use_global_device_ids=true | all-gather | bytes 737280 | tf_op jit(solution)/shard_map/all_gather | solution.py:68
  21.0 1.4 pad_maximum_fusion.4
  25.5 10.4 %all-to-all-start = ((s32[32,1,129]{2,1,0:T(1,128)}), s32[32,1,129]{2,1,0:T(1,128)S(1)}, u32[]{:S(2)}, u32[]{:S(2)}) async-start(s32[32,1,129]{2,1,0:T(1,128)} %all_to_all.17), calls=%async_computation | async-start | bytes 65536 | tf_op jit(solution)/shard_map/all_to_all | solution.py:100
  35.9 1.3 constant_dynamic-slice_fusion
  37.2 1.6 broadcast_in_dim.96
  38.8 2.8 scatter_fusion
  41.6 1.6 all-to-all-done
  43.2 5.8 %all-to-all-start.1 = ((bf16[32,128,256]{2,1,0:T(8,128)(2,1)}), bf16[32,128,256]{2,1,0:T(8,128)(2,1)S(1)}, u32[]{:S(2)}, u32[]{:S(2)}) async-start(bf16[32,128,256]{2,1,0:T(8,128)(2,1)} %scatter_fusion), calls=%async_computation.1 | async-start | bytes 4194304 | tf_op jit(solution)/shard_map/all_to_all | solution.py:99
  50.4 33.9 %all-to-all-done.1 = bf16[32,128,256]{2,1,0:T(8,128)(2,1)S(1)} async-done(((bf16[32,128,256]{2,1,0:T(8,128)(2,1)}), bf16[32,128,256]{2,1,0:T(8,128)(2,1)S(1)}, u32[]{:S(2)}, u32[]{:S(2)}) %all-to-all-start.1) | async-done | bytes 2097184 | tf_op jit(solution)/shard_map/all_to_all | solution.py:99
  84.2 1.5 gather_fusion
  87.1 45.3 %all-gather.9.cloned.1.call-done = bf16[14,128,1024]{2,1,0:T(8,128)(2,1)} async-done(((bf16[14,128,256]{2,1,0:T(8,128)(2,1)}), bf16[14,128,1024]{2,1,0:T(8,128)(2,1)}) %all-gather.9.cloned.1.call-update) | async-done | bytes 3670032 | tf_op jit(solution)/shard_map/all_gather | solution.py:109
  133.0 3.3 convolution_convert_fusion.1
  138.2 3.3 convolution_convert_fusion
  143.5 3.3 convolution_convert_fusion.2
  147.9 7.9 %while.41 = (s32[]{:T(128)}, bf16[2,896,64]{1,2,0:T(8,128)(2,1)S(1)}, s32[2,896]{1,0:T(2,128)S(1)}, s32[14,128]{1,0:T(8,128)S(1)}, bf16[2,896,64]{2,1,0:T(8,128)...) while((s32[]{:T(128)}, bf16[2,896,64]{1,2,0:T(8,128)(2,1)S(1)}, ...), condition=%wide.region_7.8_spmd, body=%wide.region_4.7_spmd.sunk | while | flops 425548032 | bytes 20567648 | solution.py:33
  150.5 1.5 fusion.111
  152.0 1.2 fusion.109
  154.3 1.5 fusion.111
  157.7 7.7 %while.42 = (s32[]{:T(128)}, bf16[2,896,64]{1,2,0:T(8,128)(2,1)S(1)}, s32[2,896]{1,0:T(2,128)S(1)}, s32[14,128]{1,0:T(8,128)S(1)}, bf16[2,896,64]{2,1,0:T(8,128)...) while((s32[]{:T(128)}, bf16[2,896,64]{1,2,0:T(8,128)(2,1)S(1)}, ...), condition=%wide.region_11.12_spmd, body=%wide.region_8.11_spmd.sunk | while | flops 425548032 | bytes 20567648 | solution.py:33
  157.7 1.2 fusion.114
  160.0 1.5 fusion.116
  161.6 1.2 fusion.114
  163.8 1.5 fusion.116
  166.5 19.4 %while.43 = (s32[]{:T(128)}, bf16[2,896,64]{1,2,0:T(8,128)(2,1)S(1)}, s32[2,896]{1,0:T(2,128)S(1)}, s32[14,128]{1,0:T(8,128)S(1)}, bf16[2,896,64]{2,1,0:T(8,128)...) while((s32[]{:T(128)}, bf16[2,896,64]{1,2,0:T(8,128)(2,1)S(1)}, ...), condition=%wide.region_15.16_spmd, body=%wide.region_12.15_spmd.sunk | while | flops 425548032 | bytes 20567648 | solution.py:33
  166.6 1.2 fusion.119
  168.8 1.5 fusion.121
  170.4 1.2 fusion.119
  172.7 1.5 fusion.121
  187.1 7.7 %while.44 = (s32[]{:T(128)}, bf16[2,896,64]{1,2,0:T(8,128)(2,1)S(1)}, s32[2,896]{1,0:T(2,128)S(1)}, s32[14,128]{1,0:T(8,128)S(1)}, bf16[2,896,64]{2,1,0:T(8,128)...) while((s32[]{:T(128)}, bf16[2,896,64]{1,2,0:T(8,128)(2,1)S(1)}, ...), condition=%wide.region_19.20_spmd, body=%wide.region_16.19_spmd.sunk | while | flops 425548032 | bytes 20567648 | solution.py:33
  189.4 1.5 fusion.126
  191.0 1.2 fusion.124
  193.3 1.5 fusion.126
  196.7 3.7 %all-to-all-start.2 = ((bf16[14,4,32,256]{3,2,0,1:T(8,128)(2,1)}), bf16[14,4,32,256]{3,2,0,1:T(8,128)(2,1)S(1)}, u32[]{:S(2)}, u32[]{:S(2)}) async-start(bf16[14,4,32,256]{3,2,0,1:T(8,128)(2,1)} %copy.102), calls=%async_computation.2 | async-start | bytes 1835008 | tf_op jit(solution)/shard_map/all_to_all | solution.py:133
  200.4 11.1 %all-to-all-done.2 = bf16[14,4,32,256]{3,2,0,1:T(8,128)(2,1)S(1)} async-done(((bf16[14,4,32,256]{3,2,0,1:T(8,128)(2,1)}), bf16[14,4,32,256]{3,2,0,1:T(8,128)(2,1)S(1)}, u32[]{:S(2)}, u32[]{:S(2)}) %all-to-all-start.2) | async-done | bytes 917536 | tf_op jit(solution)/shard_map/all_to_all | solution.py:133
  211.5 1.5 convolution_convert_fusion.6
  213.0 1.5 convolution_convert_fusion.5
  214.5 1.5 convolution_convert_fusion.4
  216.0 2.2 fusion.74
  218.5 21.7 %fusion.35 = bf16[14,32,4096]{2,1,0:T(8,128)(2,1)S(1)} fusion(bf16[1024,8192]{1,0:T(8,128)(2,1)} %all-gather.11.cloned.1.call-done, f32[14,32,1024]{2,1,0:T(8,128)S(1)} %get-tuple-element.375, f32[1024]{0:T(1024)S(1)} %copy-done.15, f32[1024]{0:T(1024)S(1)} %copy-done.16, f32[14,32]{1,0:T(8,128)S(1)} %add_rsqrt_fusion.1, ...), kind=kOutput, calls=%fused_computation.59 | convolution fusion | flops 3879665664 | bytes 13905408 | tf_op jit(solution)/shard_map/pid,du->piu/dot_general | solution.py:156
  243.7 1.7 fusion.75
  246.9 1.5 broadcast_select_fusion
  248.4 10.6 %all-to-all-start.3 = ((bf16[32,32,1024]{2,1,0:T(8,128)(2,1)}), bf16[32,32,1024]{2,1,0:T(8,128)(2,1)S(1)}, u32[]{:S(2)}, u32[]{:S(2)}) async-start(bf16[32,32,1024]{2,1,0:T(8,128)(2,1)} %broadcast_select_fusion), calls=%async_computation.3 | async-start | bytes 4194304 | tf_op jit(solution)/shard_map/all_to_all | solution.py:178
  259.1 28.5 %all-to-all-done.3 = bf16[32,32,1024]{2,1,0:T(8,128)(2,1)S(1)} async-done(((bf16[32,32,1024]{2,1,0:T(8,128)(2,1)}), bf16[32,32,1024]{2,1,0:T(8,128)(2,1)S(1)}, u32[]{:S(2)}, u32[]{:S(2)}) %all-to-all-start.3) | async-done | bytes 2097184 | tf_op jit(solution)/shard_map/all_to_all | solution.py:178
  287.6 1.5 gather_fusion.3
  289.2 1.3 pad_maximum_fusion
  290.6 3.6 %copy.97 = bf16[1792,2,256]{2,1,0:T(2,128)(2,1)} copy(bf16[1792,2,256]{0,2,1:T(8,128)(2,1)S(1)} %pad_maximum_fusion) | data formatting | bytes 3670016
  294.1 35.4 %all-gather.13.cloned.1.call-done = bf16[14,128,1024]{2,1,0:T(8,128)(2,1)} async-done(((bf16[14,32,1024]{2,1,0:T(8,128)(2,1)}), bf16[14,128,1024]{2,1,0:T(8,128)(2,1)}) %all-gather.13.cloned.1.call-update) | async-done | bytes 3670032 | tf_op jit(solution)/shard_map/all_gather | solution.py:180
  329.5 4.2 %copy.141 = bf16[1792,1024]{1,0:T(8,128)(2,1)} copy(bf16[1792,1024]{1,0:T(8,128)(2,1)} %bitcast.187) | data formatting | bytes 7340032
  (124 shorter events, 34.7 us)
Async XLA Ops:
  7.2 78.6 %all-gather.7.cloned.1.call-start = ((), (), s32[]{:S(2)}) async-start(), calls=%async_computation.4 | async-start | bytes 3784704 | tf_op jit(solution)/shard_map/all_gather | solution.py:74
  23.3 19.9 %copy-start.9 = (s32[14]{0:T(128)}, s32[14]{0:T(128)S(1)}, u32[]{:S(2)}) copy-start(s32[14]{0:T(128)S(1)} %compare_select_fusion.2) | copy-start | bytes 172
  25.5 17.7 %all-to-all-start = ((s32[32,1,129]{2,1,0:T(1,128)}), s32[32,1,129]{2,1,0:T(1,128)S(1)}, u32[]{:S(2)}, u32[]{:S(2)}) async-start(s32[32,1,129]{2,1,0:T(1,128)} %all_to_all.17), calls=%async_computation | async-start | bytes 65536 | tf_op jit(solution)/shard_map/all_to_all | solution.py:100
  43.2 41.0 %all-to-all-start.1 = ((bf16[32,128,256]{2,1,0:T(8,128)(2,1)}), bf16[32,128,256]{2,1,0:T(8,128)(2,1)S(1)}, u32[]{:S(2)}, u32[]{:S(2)}) async-start(bf16[32,128,256]{2,1,0:T(8,128)(2,1)} %scatter_fusion), calls=%async_computation.1 | async-start | bytes 4194304 | tf_op jit(solution)/shard_map/all_to_all | solution.py:99
  49.0 83.3 %all-gather.9.cloned.1.call-start = ((), (), s32[]{:S(2)}) async-start(), calls=%async_computation.5 | async-start | bytes 4587520 | tf_op jit(solution)/shard_map/all_gather | solution.py:109
  49.8 0.6 copy-start.12
  85.8 132.7 %all-gather.11.cloned.1.call-start = ((), (), s32[]{:S(2)}) async-start(), calls=%async_computation.6 | async-start | bytes 17301504 | tf_op jit(solution)/shard_map/all_gather | solution.py:112
  136.3 0.9 copy-start
  141.5 1.0 copy-start.2
  166.5 19.8 %copy-start.4 = (bf16[1792,64]{0,1:T(8,128)(2,1)S(1)}, bf16[1792,64]{0,1:T(8,128)(2,1)}, u32[]{:S(2)}) copy-start(bf16[1792,64]{0,1:T(8,128)(2,1)} %get-tuple-element.363) | copy-start | bytes 688132
  166.5 20.0 %copy-start.5 = (bf16[1792,64]{0,1:T(8,128)(2,1)S(1)}, bf16[1792,64]{0,1:T(8,128)(2,1)}, u32[]{:S(2)}) copy-start(bf16[1792,64]{0,1:T(8,128)(2,1)} %get-tuple-element.359) | copy-start | bytes 688132
  166.5 20.3 %copy-start.6 = (bf16[1792,64]{0,1:T(8,128)(2,1)S(1)}, bf16[1792,64]{0,1:T(8,128)(2,1)}, u32[]{:S(2)}) copy-start(bf16[1792,64]{0,1:T(8,128)(2,1)} %get-tuple-element.367) | copy-start | bytes 688132
  187.1 8.0 %copy-start.3 = (bf16[2,896,64]{2,1,0:T(8,128)(2,1)S(1)}, bf16[2,896,64]{2,1,0:T(8,128)(2,1)}, u32[]{:S(2)}) copy-start(bf16[2,896,64]{2,1,0:T(8,128)(2,1)} %copy.80) | copy-start | bytes 688132
  194.8 5.6 %copy-start.11 = (s32[32]{0:T(128)S(1)}, s32[32]{0:T(128)}, u32[]{:S(2)}) copy-start(s32[32]{0:T(128)} %get-tuple-element.292) | copy-start | bytes 388
  194.8 5.6 %copy-start.13 = (s32[32]{0:T(128)S(1)}, s32[32]{0:T(128)}, u32[]{:S(2)}) copy-start(s32[32]{0:T(128)} %copy-done.12) | copy-start | bytes 388
  196.7 14.8 %all-to-all-start.2 = ((bf16[14,4,32,256]{3,2,0,1:T(8,128)(2,1)}), bf16[14,4,32,256]{3,2,0,1:T(8,128)(2,1)S(1)}, u32[]{:S(2)}, u32[]{:S(2)}) async-start(bf16[14,4,32,256]{3,2,0,1:T(8,128)(2,1)} %copy.102), calls=%async_computation.2 | async-start | bytes 1835008 | tf_op jit(solution)/shard_map/all_to_all | solution.py:133
  200.4 18.1 %copy-start.15 = (f32[1024]{0:T(1024)S(1)}, f32[1024]{0:T(1024)}, u32[]{:S(2)}) copy-start(f32[1024]{0:T(1024)} %param.33) | copy-start | bytes 12292
  200.4 18.1 %copy-start.16 = (f32[1024]{0:T(1024)S(1)}, f32[1024]{0:T(1024)}, u32[]{:S(2)}) copy-start(f32[1024]{0:T(1024)} %param.32) | copy-start | bytes 12292
  218.5 21.7 %copy-start.14 = (bf16[1024,8192]{1,0:T(8,128)(2,1)S(1)}, bf16[1024,8192]{1,0:T(8,128)(2,1)}, u32[]{:S(2)}) copy-start(bf16[1024,8192]{1,0:T(8,128)(2,1)} %all-gather.11.cloned.1.call-done) | copy-start | bytes 50331652
  243.7 2.1 copy-start.7
  243.7 2.1 copy-start.8
  246.2 12.9 %copy-start.10 = (s32[14]{0:T(128)S(1)}, s32[14]{0:T(128)}, u32[]{:S(2)}) copy-start(s32[14]{0:T(128)} %copy-done.9) | copy-start | bytes 172
  248.4 40.8 %copy-start.1 = (bf16[1792,256]{0,1:T(8,128)(2,1)S(1)}, bf16[1792,256]{0,1:T(8,128)(2,1)}, u32[]{:S(2)}) copy-start(bf16[1792,256]{0,1:T(8,128)(2,1)} %copy-done) | copy-start | bytes 2752516
  248.4 39.2 %all-to-all-start.3 = ((bf16[32,32,1024]{2,1,0:T(8,128)(2,1)}), bf16[32,32,1024]{2,1,0:T(8,128)(2,1)S(1)}, u32[]{:S(2)}, u32[]{:S(2)}) async-start(bf16[32,32,1024]{2,1,0:T(8,128)(2,1)} %broadcast_select_fusion), calls=%async_computation.3 | async-start | bytes 4194304 | tf_op jit(solution)/shard_map/all_to_all | solution.py:178
  259.0 70.5 %all-gather.13.cloned.1.call-start = ((), (), s32[]{:S(2)}) async-start(), calls=%async_computation.7 | async-start | bytes 4587520 | tf_op jit(solution)/shard_map/all_gather | solution.py:180
Sparse Core Ops, SparseCore 0:
  22.5 62.8 all-gather.6
  87.6 44.6 all-gather.8
  135.2 75.3 all-gather.10
  289.3 40.1 all-gather.12
